TPU v7x, 32 devices: a whole 2x2x4 slice. The times are simulated.
32 devices in a mesh: occ: 4 (over z), aux: 4 (over x, core), vir: 2 (over y).
Axes of the slice: x: 2, y: 2, z: 4, core: 2. Of those that a mesh axis runs over, the one named last changes fastest.
Arguments:
- integrals: bfloat16 [4, 2048, 4096], P('occ', 'vir', 'aux'), may hold values from -0.65625 to 0.65625
- occ_energy: float32 [4], replicated, may hold values from -2 to -0.5
- vir_energy: float32 [2048], replicated, may hold values from 0.25 to 3
Outputs:
- lagrangian: bfloat16 [4, 2048, 4096], P('occ', 'vir', 'aux')
All inputs are finite; a program needn't handle non-finite values.
Results may differ from a plain program's by a relative error of at most 0.0039.
Values may be sent and summed in bfloat16 or wider, within the bound.
No kernel may reach another device: no remote copies, remote signals or barrier semaphores. Data moves between devices by JAX's collectives and lax.ppermute only.
A program may use at most 64 MiB of HBM per device.

v0:
```python
import jax
import jax.numpy as jnp
from jax import lax
from jax.sharding import PartitionSpec as P

CHUNKS = 4
AUX_BY_PERMUTE = False
Z_GATED = False


def shifted_2(value, axis, by):
    count = lax.axis_size(axis)
    return lax.ppermute(value, axis, [(i, (i + by) % count) for i in range(count)])


def general_plan(integrals, occ_energy, vir_energy):
    row_count = integrals.shape[0]
    vir_width = integrals.shape[1]
    cycle_size = lax.axis_size("occ")
    position = lax.axis_index("occ")
    own_level = lax.dynamic_slice_in_dim(occ_energy, position * row_count, row_count)
    partner_level = lax.dynamic_slice_in_dim(
        occ_energy, (position - 2) % cycle_size * row_count, row_count
    )
    local_vir = lax.dynamic_slice_in_dim(vir_energy, lax.axis_index("vir") * vir_width, vir_width)
    shifted = shifted_2(integrals, "occ", 2)
    partner = lax.all_gather(shifted, "vir", axis=1, tiled=True)
    virtuals = partner.shape[1]
    pair_level = own_level + partner_level
    share_rows = virtuals // lax.axis_size("aux")
    partial_value = lax.psum_scatter(
        jnp.einsum("nbq,naq->bna", partner, integrals, preferred_element_type=jnp.float32),
        "aux",
        scatter_dimension=0,
        tiled=True,
    )
    first_row = lax.axis_index("aux") * share_rows
    vir_rows = lax.dynamic_slice_in_dim(vir_energy, first_row, share_rows)
    amplitudes = (
        partial_value
        / (pair_level[None, :, None] - vir_rows[:, None, None] - local_vir[None, None, :])
    ).astype(jnp.bfloat16)
    portion = lax.all_gather(amplitudes, "aux", axis=0, tiled=True)
    own_part = jnp.einsum("bna,nbq->naq", portion, partner, preferred_element_type=jnp.float32)
    rows_back = jnp.einsum("bna,naq->nbq", portion, integrals, preferred_element_type=jnp.float32)
    owned = lax.psum_scatter(rows_back, "vir", scatter_dimension=1, tiled=True)
    returned = shifted_2(owned, "occ", -2)
    return (own_part + returned).astype(jnp.bfloat16)


def xor_pairs(count, step):
    return [(j, j ^ step) for j in range(count)]


def aux_reduce_scatter(x):
    count = lax.axis_size("aux")
    k = lax.axis_index("aux")
    first = 0
    step = 1
    while step < count:
        half = x.shape[0] // 2
        bit = k // step % 2
        keep = lax.dynamic_slice_in_dim(x, bit * half, half, 0)
        send = lax.dynamic_slice_in_dim(x, (1 - bit) * half, half, 0)
        x = keep + lax.ppermute(send, "aux", xor_pairs(count, step))
        first = first + bit * half
        step *= 2
    return (x, first)


def aux_all_gather(x):
    count = lax.axis_size("aux")
    k = lax.axis_index("aux")
    step = count // 2
    while step >= 1:
        bit = k // step % 2
        other = lax.ppermute(x, "aux", xor_pairs(count, step))
        x = jnp.where(bit == 0, jnp.concatenate([x, other]), jnp.concatenate([other, x]))
        step //= 2
    return x


def paired_plan(integrals, occ_energy, vir_energy):
    own = integrals[0]
    vir_rows, _ = own.shape
    cycle_size = lax.axis_size("occ")
    position = lax.axis_index("occ")
    pair_level = occ_energy[position] + occ_energy[(position - 2) % cycle_size]
    vir_pos = lax.axis_index("vir")
    vir_count = lax.axis_size("vir")
    aux_count = lax.axis_size("aux")
    share = vir_rows // aux_count
    width = vir_rows // CHUNKS
    if not AUX_BY_PERMUTE:
        first_row = lax.axis_index("aux") * share

    def forward(c, arrived):
        if vir_count == 2:
            mate = shifted_2(arrived, "vir", 1)
            block = jnp.concatenate([arrived, mate])
            cols = [vir_pos, 1 - vir_pos]
        else:
            block = lax.all_gather(arrived, "vir", axis=0, tiled=True)
            cols = list(range(vir_count))
        col_level = jnp.concatenate(
            [lax.dynamic_slice_in_dim(vir_energy, w * vir_rows + c * width, width) for w in cols]
        )
        return (block, col_level)

    def reduce(block):
        partial = jnp.einsum("aq,bq->ab", own, block, preferred_element_type=jnp.float32)
        if AUX_BY_PERMUTE:
            return aux_reduce_scatter(partial)
        return (lax.psum_scatter(partial, "aux", scatter_dimension=0, tiled=True), first_row)

    def amplitudes_of(summed, first, col_level):
        row_level = lax.dynamic_slice_in_dim(vir_energy, vir_pos * vir_rows + first, share)
        amplitudes = (summed / (pair_level - row_level[:, None] - col_level[None, :])).astype(
            jnp.bfloat16
        )
        if AUX_BY_PERMUTE:
            return aux_all_gather(amplitudes)
        return lax.all_gather(amplitudes, "aux", axis=0, tiled=True)

    arrived = [None] * CHUNKS
    blocks = [None] * CHUNKS
    levels = [None] * CHUNKS
    summed = [None] * CHUNKS
    firsts = [None] * CHUNKS
    gathered = [None] * CHUNKS
    total = None
    for c in range(CHUNKS if not Z_GATED else 0):
        arrived[c] = shifted_2(own[c * width : (c + 1) * width], "occ", 2)
    for t in range(CHUNKS + 4):
        piece = own[t * width : (t + 1) * width] if Z_GATED and t < CHUNKS else None
        if t > 0:
            gate = {"arrived": arrived[t - 1] if t - 1 < CHUNKS else None}
            if piece is not None:
                gate["piece"] = piece
            if 0 <= t - 2 < CHUNKS:
                gate["block"] = blocks[t - 2]
            if 0 <= t - 3 < CHUNKS:
                gate["summed"] = summed[t - 3]
            if 0 <= t - 4 < CHUNKS:
                gate["gathered"] = gathered[t - 4]
            if total is not None:
                gate["total"] = total
            gate = lax.optimization_barrier(gate)
            if piece is not None:
                piece = gate["piece"]
            if t - 1 < CHUNKS:
                arrived[t - 1] = gate["arrived"]
            if 0 <= t - 2 < CHUNKS:
                blocks[t - 2] = gate["block"]
            if 0 <= t - 3 < CHUNKS:
                summed[t - 3] = gate["summed"]
            if 0 <= t - 4 < CHUNKS:
                gathered[t - 4] = gate["gathered"]
            if total is not None:
                total = gate["total"]
        if piece is not None:
            arrived[t] = shifted_2(piece, "occ", 2)
        c = t - 1
        if 0 <= c < CHUNKS:
            blocks[c], levels[c] = forward(c, arrived[c])
        c = t - 2
        if 0 <= c < CHUNKS:
            summed[c], firsts[c] = reduce(blocks[c])
        c = t - 3
        if 0 <= c < CHUNKS:
            gathered[c] = amplitudes_of(summed[c], firsts[c], levels[c])
        c = t - 4
        if 0 <= c < CHUNKS:
            term = jnp.dot(gathered[c], blocks[c], preferred_element_type=jnp.float32)
            total = term if total is None else total + term
    gamma_own = total
    gamma_back = total
    return (gamma_own + gamma_back).astype(jnp.bfloat16)[None]


def on_device(integrals, occ_energy, vir_energy):
    cycle_size = lax.axis_size("occ")
    if integrals.shape[0] == 1 and 4 % cycle_size == 0 and (integrals.shape[1] % (CHUNKS * 8) == 0):
        return paired_plan(integrals, occ_energy, vir_energy)
    return general_plan(integrals, occ_energy, vir_energy)


def solution(mesh):
    placed = (P("occ", "vir", "aux"), P(), P())
    return jax.shard_map(
        on_device, mesh=mesh, in_specs=placed, out_specs=P("occ", "vir", "aux"), check_vma=False
    )
```

profile of v0, /device:TPU:0, one launch (start us, length us, event | category | flops | bytes accessed | tf_op | source)
XLA Modules:
  0.0 284.6 jit_solution(10130402411361232367)
XLA Ops:
  6.5 2.7 slice_bitcast_fusion
  9.2 4.0 %collective-permute-start.3 = (bf16[256,1024]{1,0:T(8,128)(2,1)S(1)}, bf16[256,1024]{1,0:T(8,128)(2,1)S(1)}, u32[]{:S(2)}, u32[]{:S(2)}) collective-permute-start(bf16[256,1024]{1,0:T(8,128)(2,1)S(1)} %get-tuple-element.41), channel_id=1, source_target_pairs={{0,16},{8,24},{16,0},{24,8},{1,17},{9,25},{17,1},{25,9},{2,18},{10... | collective-permute-start | bytes 1572872 | tf_op jit(solution)/shard_map/ppermute | solution.py:13
  13.3 23.2 %collective-permute-done.3 = bf16[256,1024]{1,0:T(8,128)(2,1)S(1)} collective-permute-done((bf16[256,1024]{1,0:T(8,128)(2,1)S(1)}, bf16[256,1024]{1,0:T(8,128)(2,1)S(1)}, u32[]{:S(2)}, u32[]{:S(2)}) %collective-permute-start.3) | collective-permute-done | bytes 524320 | tf_op jit(solution)/shard_map/ppermute | solution.py:13
  38.0 11.5 %collective-permute-done.4 = bf16[256,1024]{1,0:T(8,128)(2,1)S(1)} collective-permute-done((bf16[256,1024]{1,0:T(8,128)(2,1)S(1)}, bf16[256,1024]{1,0:T(8,128)(2,1)S(1)}, u32[]{:S(2)}, u32[]{:S(2)}) %collective-permute-start.4) | collective-permute-done | bytes 524320 | tf_op jit(solution)/shard_map/ppermute | solution.py:13
  49.6 13.1 %collective-permute-done.2 = bf16[256,1024]{1,0:T(8,128)(2,1)S(1)} collective-permute-done((bf16[256,1024]{1,0:T(8,128)(2,1)S(1)}, bf16[256,1024]{1,0:T(8,128)(2,1)S(1)}, u32[]{:S(2)}, u32[]{:S(2)}) %collective-permute-start.2) | collective-permute-done | bytes 524320 | tf_op jit(solution)/shard_map/ppermute | solution.py:13
  62.7 2.6 fusion.8
  68.2 9.3 %collective-permute-done.5 = bf16[256,1024]{1,0:T(8,128)(2,1)} collective-permute-done((bf16[256,1024]{1,0:T(8,128)(2,1)S(1)}, bf16[256,1024]{1,0:T(8,128)(2,1)}, u32[]{:S(2)}, u32[]{:S(2)}) %collective-permute-start.5) | collective-permute-done | bytes 524320 | tf_op jit(solution)/shard_map/ppermute | solution.py:13
  78.5 11.8 %collective-permute-done.1 = bf16[256,1024]{1,0:T(8,128)(2,1)S(1)} collective-permute-done((bf16[256,1024]{1,0:T(8,128)(2,1)}, bf16[256,1024]{1,0:T(8,128)(2,1)S(1)}, u32[]{:S(2)}, u32[]{:S(2)}) %collective-permute-start.1) | collective-permute-done | bytes 524320 | tf_op jit(solution)/shard_map/ppermute | solution.py:13
  90.4 4.3 %reduce-scatter.5.cloned.1.call-done = f32[256,512]{0,1:T(8,128)} async-done(((f32[1024,512]{0,1:T(8,128)}), f32[256,512]{0,1:T(8,128)}) %reduce-scatter.5.cloned.1.call-update) | async-done | bytes 524304 | tf_op jit(solution)/shard_map/reduce_scatter | solution.py:114
  96.7 4.2 %fusion.11 = f32[1024,512]{0,1:T(8,128)} fusion(bf16[512,1024]{1,0:T(8,128)(2,1)S(1)} %pad_maximum_fusion.1, bf16[1,1024,1024]{2,1,0:T(8,128)(2,1)} %param.3), kind=kOutput, calls=%fused_computation.11 | convolution fusion | flops 1073741824 | bytes 5242880 | tf_op jit(solution)/shard_map/aq,bq->ab/dot_general | solution.py:111
  104.9 9.8 %collective-permute-done.6 = bf16[256,1024]{1,0:T(8,128)(2,1)S(1)} collective-permute-done((bf16[256,1024]{1,0:T(8,128)(2,1)S(1)}, bf16[256,1024]{1,0:T(8,128)(2,1)S(1)}, u32[]{:S(2)}, u32[]{:S(2)}) %collective-permute-start.6) | collective-permute-done | bytes 524320 | tf_op jit(solution)/shard_map/ppermute | solution.py:13
  115.8 12.5 %collective-permute-done = bf16[256,1024]{1,0:T(8,128)(2,1)} collective-permute-done((bf16[256,1024]{1,0:T(8,128)(2,1)}, bf16[256,1024]{1,0:T(8,128)(2,1)}, u32[]{:S(2)}, u32[]{:S(2)}) %collective-permute-start) | collective-permute-done | bytes 524320 | tf_op jit(solution)/shard_map/ppermute | solution.py:13
  128.4 19.4 %reduce-scatter.7.cloned.1.call-done = f32[256,512]{0,1:T(8,128)} async-done(((f32[1024,512]{0,1:T(8,128)}), f32[256,512]{0,1:T(8,128)}) %reduce-scatter.7.cloned.1.call-update) | async-done | bytes 524304 | tf_op jit(solution)/shard_map/reduce_scatter | solution.py:114
  149.8 4.2 %fusion.14 = f32[1024,512]{0,1:T(8,128)} fusion(bf16[512,1024]{1,0:T(8,128)(2,1)S(1)} %pad_maximum_fusion.2, bf16[1,1024,1024]{2,1,0:T(8,128)(2,1)} %param.3), kind=kOutput, calls=%fused_computation.12 | convolution fusion | flops 1073741824 | bytes 5242880 | tf_op jit(solution)/shard_map/aq,bq->ab/dot_general | solution.py:111
  155.6 4.5 %fusion.23 = f32[1024,1024]{1,0:T(8,128)} fusion(bf16[1024,512]{0,1:T(8,128)(2,1)} %all-gather.5.cloned.1.call-done, bf16[512,1024]{1,0:T(8,128)(2,1)S(1)} %pad_maximum_fusion), kind=kOutput, calls=%fused_computation.34 | convolution fusion | flops 1073741824 | bytes 6291456 | tf_op jit(solution)/shard_map/dot_general | solution.py:174
  160.1 7.9 %collective-permute-done.7 = bf16[256,1024]{1,0:T(8,128)(2,1)S(1)} collective-permute-done((bf16[256,1024]{1,0:T(8,128)(2,1)}, bf16[256,1024]{1,0:T(8,128)(2,1)S(1)}, u32[]{:S(2)}, u32[]{:S(2)}) %collective-permute-start.7) | collective-permute-done | bytes 524320 | tf_op jit(solution)/shard_map/ppermute | solution.py:13
  169.1 31.4 %reduce-scatter.9.cloned.1.call-done = f32[256,512]{0,1:T(8,128)} async-done(((f32[1024,512]{0,1:T(8,128)}), f32[256,512]{0,1:T(8,128)}) %reduce-scatter.9.cloned.1.call-update) | async-done | bytes 524304 | tf_op jit(solution)/shard_map/reduce_scatter | solution.py:114
  202.6 4.2 %fusion.17 = f32[1024,512]{0,1:T(8,128)} fusion(bf16[512,1024]{1,0:T(8,128)(2,1)S(1)} %pad_maximum_fusion.3, bf16[1,1024,1024]{2,1,0:T(8,128)(2,1)} %param.3), kind=kOutput, calls=%fused_computation.13 | convolution fusion | flops 1073741824 | bytes 5242880 | tf_op jit(solution)/shard_map/aq,bq->ab/dot_general | solution.py:111
  210.3 2.9 %add.120 = f32[1024,1024]{1,0:T(8,128)} add(f32[1024,1024]{1,0:T(8,128)S(1)} %copy-done, f32[1024,1024]{1,0:T(8,128)S(1)} %fusion.24) | non-fusion elementwise | flops 1048576 | bytes 12582912 | tf_op jit(solution)/shard_map/add | solution.py:175
  213.2 6.3 %all-gather.9.cloned.1.call-done = bf16[1024,512]{0,1:T(8,128)(2,1)} async-done(((bf16[256,512]{0,1:T(8,128)(2,1)}), bf16[1024,512]{0,1:T(8,128)(2,1)}) %all-gather.9.cloned.1.call-update) | async-done | bytes 1048592 | tf_op jit(solution)/shard_map/all_gather | solution.py:123
  219.5 34.1 %reduce-scatter.11.cloned.1.call-done = f32[256,512]{0,1:T(8,128)} async-done(((f32[1024,512]{0,1:T(8,128)}), f32[256,512]{0,1:T(8,128)}) %reduce-scatter.11.cloned.1.call-update) | async-done | bytes 524304 | tf_op jit(solution)/shard_map/reduce_scatter | solution.py:114
  255.6 5.5 %convolution_add_fusion = f32[1024,1024]{1,0:T(8,128)} fusion(f32[1024,1024]{1,0:T(8,128)} %add.120, bf16[1024,512]{0,1:T(8,128)(2,1)S(1)} %copy-done.1, bf16[512,1024]{1,0:T(8,128)(2,1)S(1)} %pad_maximum_fusion.2), kind=kOutput, calls=%fused_computation.1 | convolution fusion | flops 1074790400 | bytes 10485760 | tf_op jit(solution)/shard_map/dot_general | solution.py:174
  261.1 11.5 %all-gather.11.cloned.1.call-done = bf16[1024,512]{0,1:T(8,128)(2,1)} async-done(((bf16[256,512]{0,1:T(8,128)(2,1)}), bf16[1024,512]{0,1:T(8,128)(2,1)}) %all-gather.11.cloned.1.call-update) | async-done | bytes 1048592 | tf_op jit(solution)/shard_map/all_gather | solution.py:123
  272.6 5.1 %fusion.20 = bf16[1,1024,1024]{2,1,0:T(8,128)(2,1)} fusion(f32[1024,1024]{1,0:T(8,128)} %convolution_add_fusion, bf16[1024,512]{0,1:T(8,128)(2,1)} %all-gather.11.cloned.1.call-done, bf16[512,1024]{1,0:T(8,128)(2,1)S(1)} %copy-done.5), kind=kOutput, calls=%fused_computation.14 | convolution fusion | flops 1076887552 | bytes 8388608 | tf_op jit(solution)/shard_map/dot_general | solution.py:174
  (58 shorter events, 23.6 us)
Async XLA Ops:
  6.5 88.2 %reduce-scatter.5.cloned.1.call-start = ((), (), s32[]{:S(2)}) async-start(), calls=%async_computation.4 | async-start | bytes 2621440 | tf_op jit(solution)/shard_map/reduce_scatter | solution.py:114
  9.2 53.4 %copy-start.2 = (bf16[1,1024,1024]{2,1,0:T(8,128)(2,1)S(1)}, bf16[1,1024,1024]{2,1,0:T(8,128)(2,1)}, u32[]{:S(2)}) copy-start(bf16[1,1024,1024]{2,1,0:T(8,128)(2,1)} %param.3) | copy-start | bytes 6291460
  9.2 27.2 %collective-permute-start.3 = (bf16[256,1024]{1,0:T(8,128)(2,1)S(1)}, bf16[256,1024]{1,0:T(8,128)(2,1)S(1)}, u32[]{:S(2)}, u32[]{:S(2)}) collective-permute-start(bf16[256,1024]{1,0:T(8,128)(2,1)S(1)} %get-tuple-element.41), channel_id=1, source_target_pairs={{0,16},{8,24},{16,0},{24,8},{1,17},{9,25},{17,1},{25,9},{2,18},{10... | collective-permute-start | bytes 1572872 | tf_op jit(solution)/shard_map/ppermute | solution.py:13
  36.4 13.1 %collective-permute-start.4 = (bf16[256,1024]{1,0:T(8,128)(2,1)S(1)}, bf16[256,1024]{1,0:T(8,128)(2,1)S(1)}, u32[]{:S(2)}, u32[]{:S(2)}) collective-permute-start(bf16[256,1024]{1,0:T(8,128)(2,1)S(1)} %collective-permute-done.3), channel_id=1, source_target_pairs={{0,1},{1,0},{2,3},{3,2},{4,5},{5,4},{6,7},{7,6},{8,9},{9,8},{10,11... | collective-permute-start | bytes 1572872 | tf_op jit(solution)/shard_map/ppermute | solution.py:13
  38.0 24.7 %collective-permute-start.2 = (bf16[256,1024]{1,0:T(8,128)(2,1)S(1)}, bf16[256,1024]{1,0:T(8,128)(2,1)S(1)}, u32[]{:S(2)}, u32[]{:S(2)}) collective-permute-start(bf16[256,1024]{1,0:T(8,128)(2,1)S(1)} %get-tuple-element.42), channel_id=1, source_target_pairs={{0,16},{8,24},{16,0},{24,8},{1,17},{9,25},{17,1},{25,9},{2,18},{10... | collective-permute-start | bytes 1572872 | tf_op jit(solution)/shard_map/ppermute | solution.py:13
  65.3 2.7 copy-start.7
  65.3 63.1 %all-gather.5.cloned.1.call-start = ((), (), s32[]{:S(2)}) async-start(), calls=%async_computation.5 | async-start | bytes 1310720 | tf_op jit(solution)/shard_map/all_gather | solution.py:123
  65.4 12.1 %collective-permute-start.5 = (bf16[256,1024]{1,0:T(8,128)(2,1)S(1)}, bf16[256,1024]{1,0:T(8,128)(2,1)}, u32[]{:S(2)}, u32[]{:S(2)}) collective-permute-start(bf16[256,1024]{1,0:T(8,128)(2,1)S(1)} %collective-permute-done.2), channel_id=1, source_target_pairs={{0,1},{1,0},{2,3},{3,2},{4,5},{5,4},{6,7},{7,6},{8,9},{9,8},{10,11... | collective-permute-start | bytes 1572872 | tf_op jit(solution)/shard_map/ppermute | solution.py:13
  66.2 24.2 %collective-permute-start.1 = (bf16[256,1024]{1,0:T(8,128)(2,1)}, bf16[256,1024]{1,0:T(8,128)(2,1)S(1)}, u32[]{:S(2)}, u32[]{:S(2)}) collective-permute-start(bf16[256,1024]{1,0:T(8,128)(2,1)} %get-tuple-element.43), channel_id=1, source_target_pairs={{0,16},{8,24},{16,0},{24,8},{1,17},{9,25},{17,1},{25,9},{2,18},{10... | collective-permute-start | bytes 1572872 | tf_op jit(solution)/shard_map/ppermute | solution.py:13
  90.4 10.6 %copy-start.6 = (bf16[256,1024]{1,0:T(8,128)(2,1)}, bf16[256,1024]{1,0:T(8,128)(2,1)S(1)}, u32[]{:S(2)}) copy-start(bf16[256,1024]{1,0:T(8,128)(2,1)S(1)} %collective-permute-done.1) | copy-start | bytes 1572868
  96.6 51.2 %reduce-scatter.7.cloned.1.call-start = ((), (), s32[]{:S(2)}) async-start(), calls=%async_computation.6 | async-start | bytes 2621440 | tf_op jit(solution)/shard_map/reduce_scatter | solution.py:114
  100.9 68.2 %all-gather.7.cloned.1.call-start = ((), (), s32[]{:S(2)}) async-start(), calls=%async_computation.7 | async-start | bytes 1310720 | tf_op jit(solution)/shard_map/all_gather | solution.py:123
  101.0 13.8 %collective-permute-start.6 = (bf16[256,1024]{1,0:T(8,128)(2,1)S(1)}, bf16[256,1024]{1,0:T(8,128)(2,1)S(1)}, u32[]{:S(2)}, u32[]{:S(2)}) collective-permute-start(bf16[256,1024]{1,0:T(8,128)(2,1)S(1)} %collective-permute-done.1), channel_id=1, source_target_pairs={{0,1},{1,0},{2,3},{3,2},{4,5},{5,4},{6,7},{7,6},{8,9},{9,8},{10,11... | collective-permute-start | bytes 1572872 | tf_op jit(solution)/shard_map/ppermute | solution.py:13
  102.5 25.8 %collective-permute-start = (bf16[256,1024]{1,0:T(8,128)(2,1)}, bf16[256,1024]{1,0:T(8,128)(2,1)}, u32[]{:S(2)}, u32[]{:S(2)}) collective-permute-start(bf16[256,1024]{1,0:T(8,128)(2,1)} %get-tuple-element.44), channel_id=1, source_target_pairs={{0,16},{8,24},{16,0},{24,8},{1,17},{9,25},{17,1},{25,9},{2,18},{10... | collective-permute-start | bytes 1572872 | tf_op jit(solution)/shard_map/ppermute | solution.py:13
  149.7 50.9 %reduce-scatter.9.cloned.1.call-start = ((), (), s32[]{:S(2)}) async-start(), calls=%async_computation.8 | async-start | bytes 2621440 | tf_op jit(solution)/shard_map/reduce_scatter | solution.py:114
  154.0 65.5 %all-gather.9.cloned.1.call-start = ((), (), s32[]{:S(2)}) async-start(), calls=%async_computation.9 | async-start | bytes 1310720 | tf_op jit(solution)/shard_map/all_gather | solution.py:123
  154.0 13.9 %collective-permute-start.7 = (bf16[256,1024]{1,0:T(8,128)(2,1)}, bf16[256,1024]{1,0:T(8,128)(2,1)S(1)}, u32[]{:S(2)}, u32[]{:S(2)}) collective-permute-start(bf16[256,1024]{1,0:T(8,128)(2,1)} %collective-permute-done), channel_id=1, source_target_pairs={{0,1},{1,0},{2,3},{3,2},{4,5},{5,4},{6,7},{7,6},{8,9},{9,8},{10,11... | collective-permute-start | bytes 1572872 | tf_op jit(solution)/shard_map/ppermute | solution.py:13
  169.1 33.5 %copy-start.4 = (bf16[512,1024]{1,0:T(8,128)(2,1)}, bf16[512,1024]{1,0:T(8,128)(2,1)S(1)}, u32[]{:S(2)}) copy-start(bf16[512,1024]{1,0:T(8,128)(2,1)S(1)} %pad_maximum_fusion.3) | copy-start | bytes 3145732
  202.5 51.2 %reduce-scatter.11.cloned.1.call-start = ((), (), s32[]{:S(2)}) async-start(), calls=%async_computation.10 | async-start | bytes 2621440 | tf_op jit(solution)/shard_map/reduce_scatter | solution.py:114
  206.8 1.2 copy-start.3
  206.8 65.8 %all-gather.11.cloned.1.call-start = ((), (), s32[]{:S(2)}) async-start(), calls=%async_computation.11 | async-start | bytes 1310720 | tf_op jit(solution)/shard_map/all_gather | solution.py:123
  208.0 2.3 copy-start
  219.5 36.1 %copy-start.1 = (bf16[1024,512]{0,1:T(8,128)(2,1)S(1)}, bf16[1024,512]{0,1:T(8,128)(2,1)}, u32[]{:S(2)}) copy-start(bf16[1024,512]{0,1:T(8,128)(2,1)} %all-gather.9.cloned.1.call-done) | copy-start | bytes 3145732
  255.6 17.0 %copy-start.5 = (bf16[512,1024]{1,0:T(8,128)(2,1)S(1)}, bf16[512,1024]{1,0:T(8,128)(2,1)}, u32[]{:S(2)}) copy-start(bf16[512,1024]{1,0:T(8,128)(2,1)} %copy-done.4) | copy-start | bytes 3145732
  (1 other events, 0.9 us)
Sparse Core Ops, SparseCore 0:
  65.4 29.2 reduce-scatter.4
  96.8 16.8 all-gather.4
  116.3 31.4 reduce-scatter.6
  149.8 16.8 all-gather.6
  169.1 31.4 reduce-scatter.8
  202.6 16.8 all-gather.8
  222.2 31.4 reduce-scatter.10
  255.7 16.8 all-gather.10
where the time goes:
time: 285 us
  waiting for transfers between devices  206 us (72%)
  matrix products  31.7 us (11%)
  between operations  14.8 us (5%)
  other arithmetic  14 us (5%)
  starting transfers between devices  12.4 us (4%)
  local copies, waits for them, and re-layouts  5.35 us (2%)
    ppermute x8, waiting for transfers between devices, shifted_2(): lax.ppermute(value, axis, [(i, (i + by) % count) for i in range(count)])  99 us
    reduce_scatter x4, waiting for transfers between devices, reduce(): lax.psum_scatter(partial, 'aux', scatter_dimension=0, tiled=True)  89.4 us
    all_gather x4, waiting for transfers between devices, amplitudes_of(): return lax.all_gather(amplitudes, 'aux', axis=0, tiled=True)  17.8 us
    dot_general x4, matrix products, paired_plan(): term = jnp.dot(gathered[c], blocks[c], preferred_element_type=jnp.float32)  16.5 us
    dot_general x4, matrix products, reduce(): jnp.einsum('aq,bq->ab', own, block, preferred_element_type=jnp.float32)  15.2 us
    ppermute x8, starting transfers between devices, shifted_2(): lax.ppermute(value, axis, [(i, (i + by) % count) for i in range(count)])  11.9 us
    convert_element_type x4, other arithmetic, amplitudes_of(): (summed / (pair_level - row_level[:, None] - col_level[None, :])).astype(...  7.58 us
  transfers between devices with their start and end apart: 16, of which 14 were waited for; matrix products, arithmetic and copies ran while one was open for 11% of the time, Pallas kernels for 0%

commit v1 on v0

--- a/solution.py
+++ b/solution.py
@@ -114,13 +114,29 @@
         return (lax.psum_scatter(partial, "aux", scatter_dimension=0, tiled=True), first_row)
 
     def amplitudes_of(summed, first, col_level):
+
+        def order_scenes_over_axis(xs, device_axis):
+            all_rows = lax.axis_size(device_axis)
+            v_next = lax.axis_index(device_axis)
+            current_block, b_now, k_now = (all_rows, v_next, xs.shape[0])
+            out_arr, next_value = (xs, 1)
+            while next_value < current_block:
+                log = []
+                for it in range(current_block):
+                    log.append((it, (it - next_value) % current_block))
+                later = lax.ppermute(out_arr, device_axis, log)
+                out_arr = jnp.concatenate([out_arr, later], axis=0)
+                next_value = 2 * next_value
+            piece_out = jnp.roll(out_arr, b_now * k_now, axis=0)
+            return piece_out
+
         row_level = lax.dynamic_slice_in_dim(vir_energy, vir_pos * vir_rows + first, share)
         amplitudes = (summed / (pair_level - row_level[:, None] - col_level[None, :])).astype(
             jnp.bfloat16
         )
         if AUX_BY_PERMUTE:
             return aux_all_gather(amplitudes)
-        return lax.all_gather(amplitudes, "aux", axis=0, tiled=True)
+        return order_scenes_over_axis(amplitudes, "aux")
 
     arrived = [None] * CHUNKS
     blocks = [None] * CHUNKS

time: 285 us -> 239 us (0.84)
  waiting for transfers between devices: 206 us -> 157 us
  starting transfers between devices: 12.4 us -> 19.1 us
  matrix products: 31.7 us -> 26.1 us
    reduce_scatter x4, waiting for transfers between devices: 89.4 us -> 25.4 us  [reduce(): lax.psum_scatter(partial, 'aux', scatter_dimension=0, tiled=True)]
    ppermute x0 -> x8, waiting for transfers between devices: none -> 40.9 us  [order_scenes_over_axis(): later = lax.ppermute(out_arr, device_axis, log)]
    all_gather x4 -> x0, waiting for transfers between devices: 17.8 us -> none  [amplitudes_of(): return lax.all_gather(amplitudes, 'aux', axis=0, tiled=True)]
    ppermute x8, waiting for transfers between devices: 99 us -> 90.4 us  [shifted_2(): lax.ppermute(value, axis, [(i, (i + by) % count) for i in range(count)])]
    ppermute x0 -> x8, starting transfers between devices: none -> 7.12 us  [order_scenes_over_axis(): later = lax.ppermute(out_arr, device_axis, log)]
    concatenate x0 -> x8, other arithmetic: none -> 4.98 us  [the longest x4 4.84 us: order_scenes_over_axis(): piece_out = jnp.roll(out_arr, b_now * k_now, axis=0)]
    dot_general x4, matrix products: 16.5 us -> 12.2 us  [paired_plan(): term = jnp.dot(gathered[c], blocks[c], preferred_element_type=jnp.float32)]
    convert_element_type x4, other arithmetic: 7.58 us -> 3.69 us  [amplitudes_of(): (summed / (pair_level - row_level[:, None] - col_level[None, :])).astype(...]
  transfers between devices with their start and end apart: 16 -> 20, of which waited for: 14 -> 19; matrix products, arithmetic and copies ran while one was open for 11% -> 10% of each run, Pallas kernels for 0% -> 0%
where the time goes in v1:
time: 239 us
  waiting for transfers between devices  157 us (66%)
  matrix products  26.1 us (11%)
  starting transfers between devices  19.1 us (8%)
  other arithmetic  16.1 us (7%)
  between operations  14.5 us (6%)
  local copies, waits for them, and re-layouts  5.93 us (2%)
    ppermute x8, waiting for transfers between devices, shifted_2(): lax.ppermute(value, axis, [(i, (i + by) % count) for i in range(count)])  90.4 us
    ppermute x8, waiting for transfers between devices, order_scenes_over_axis(): later = lax.ppermute(out_arr, device_axis, log)  40.9 us
    reduce_scatter x4, waiting for transfers between devices, reduce(): lax.psum_scatter(partial, 'aux', scatter_dimension=0, tiled=True)  25.4 us
    dot_general x4, matrix products, reduce(): jnp.einsum('aq,bq->ab', own, block, preferred_element_type=jnp.float32)  13.9 us
    dot_general x4, matrix products, paired_plan(): term = jnp.dot(gathered[c], blocks[c], preferred_element_type=jnp.float32)  12.2 us
    ppermute x8, starting transfers between devices, shifted_2(): lax.ppermute(value, axis, [(i, (i + by) % count) for i in range(count)])  11.8 us
    ppermute x8, starting transfers between devices, order_scenes_over_axis(): later = lax.ppermute(out_arr, device_axis, log)  7.12 us
    concatenate x4, other arithmetic, order_scenes_over_axis(): piece_out = jnp.roll(out_arr, b_now * k_now, axis=0)  4.84 us
  transfers between devices with their start and end apart: 20, of which 19 were waited for; matrix products, arithmetic and copies ran while one was open for 10% of the time, Pallas kernels for 0%

profile of v1, /device:TPU:0, one launch (start us, length us, event | category | flops | bytes accessed | tf_op | source)
XLA Modules:
  0.0 238.5 jit_solution(9269684696717142671)
XLA Ops:
  6.5 2.8 %slice_bitcast_fusion = (bf16[256,1024]{1,0:T(8,128)(2,1)S(1)}, bf16[256,1024]{1,0:T(8,128)(2,1)S(1)}, bf16[256,1024]{1,0:T(8,128)(2,1)}, bf16[256,1024]{1,0:T(8,128)(2,1)}) fusion(bf16[1,1024,1024]{2,1,0:T(8,128)(2,1)} %param.5), kind=kLoop, calls=%fused_computation.71 | loop fusion | bytes 4194304 | tf_op jit(solution)/shard_map/slice | solution.py:149
  9.3 4.0 %collective-permute-start.3 = (bf16[256,1024]{1,0:T(8,128)(2,1)S(1)}, bf16[256,1024]{1,0:T(8,128)(2,1)S(1)}, u32[]{:S(2)}, u32[]{:S(2)}) collective-permute-start(bf16[256,1024]{1,0:T(8,128)(2,1)S(1)} %get-tuple-element.42), channel_id=1, source_target_pairs={{0,16},{8,24},{16,0},{24,8},{1,17},{9,25},{17,1},{25,9},{2,18},{10... | collective-permute-start | bytes 1572872 | tf_op jit(solution)/shard_map/ppermute | solution.py:13
  13.3 23.2 %collective-permute-done.3 = bf16[256,1024]{1,0:T(8,128)(2,1)S(1)} collective-permute-done((bf16[256,1024]{1,0:T(8,128)(2,1)S(1)}, bf16[256,1024]{1,0:T(8,128)(2,1)S(1)}, u32[]{:S(2)}, u32[]{:S(2)}) %collective-permute-start.3) | collective-permute-done | bytes 524320 | tf_op jit(solution)/shard_map/ppermute | solution.py:13
  38.1 11.5 %collective-permute-done.4 = bf16[256,1024]{1,0:T(8,128)(2,1)S(1)} collective-permute-done((bf16[256,1024]{1,0:T(8,128)(2,1)S(1)}, bf16[256,1024]{1,0:T(8,128)(2,1)S(1)}, u32[]{:S(2)}, u32[]{:S(2)}) %collective-permute-start.4) | collective-permute-done | bytes 524320 | tf_op jit(solution)/shard_map/ppermute | solution.py:13
  49.7 13.2 %collective-permute-done.2 = bf16[256,1024]{1,0:T(8,128)(2,1)} collective-permute-done((bf16[256,1024]{1,0:T(8,128)(2,1)S(1)}, bf16[256,1024]{1,0:T(8,128)(2,1)}, u32[]{:S(2)}, u32[]{:S(2)}) %collective-permute-start.2) | collective-permute-done | bytes 524320 | tf_op jit(solution)/shard_map/ppermute | solution.py:13
  66.3 11.3 %collective-permute-done.5 = bf16[256,1024]{1,0:T(8,128)(2,1)S(1)} collective-permute-done((bf16[256,1024]{1,0:T(8,128)(2,1)}, bf16[256,1024]{1,0:T(8,128)(2,1)S(1)}, u32[]{:S(2)}, u32[]{:S(2)}) %collective-permute-start.5) | collective-permute-done | bytes 524320 | tf_op jit(solution)/shard_map/ppermute | solution.py:13
  78.8 11.8 %collective-permute-done.1 = bf16[256,1024]{1,0:T(8,128)(2,1)} collective-permute-done((bf16[256,1024]{1,0:T(8,128)(2,1)}, bf16[256,1024]{1,0:T(8,128)(2,1)}, u32[]{:S(2)}, u32[]{:S(2)}) %collective-permute-start.1) | collective-permute-done | bytes 524320 | tf_op jit(solution)/shard_map/ppermute | solution.py:13
  90.6 4.3 %reduce-scatter.5.cloned.1.call-done = f32[256,512]{0,1:T(8,128)} async-done(((f32[1024,512]{0,1:T(8,128)}), f32[256,512]{0,1:T(8,128)}) %reduce-scatter.5.cloned.1.call-update) | async-done | bytes 524304 | tf_op jit(solution)/shard_map/reduce_scatter | solution.py:114
  108.9 6.0 %collective-permute-done.6 = bf16[256,1024]{1,0:T(8,128)(2,1)S(1)} collective-permute-done((bf16[256,1024]{1,0:T(8,128)(2,1)}, bf16[256,1024]{1,0:T(8,128)(2,1)S(1)}, u32[]{:S(2)}, u32[]{:S(2)}) %collective-permute-start.6) | collective-permute-done | bytes 524320 | tf_op jit(solution)/shard_map/ppermute | solution.py:13
  116.0 6.6 %collective-permute-done.8 = bf16[512,512]{0,1:T(8,128)(2,1)} collective-permute-done((bf16[512,512]{0,1:T(8,128)(2,1)S(1)}, bf16[512,512]{0,1:T(8,128)(2,1)}, u32[]{:S(2)}, u32[]{:S(2)}) %collective-permute-start.8) | collective-permute-done | bytes 524320 | tf_op jit(solution)/shard_map/ppermute | solution.py:127
  124.6 9.0 %collective-permute-done = bf16[256,1024]{1,0:T(8,128)(2,1)} collective-permute-done((bf16[256,1024]{1,0:T(8,128)(2,1)}, bf16[256,1024]{1,0:T(8,128)(2,1)}, u32[]{:S(2)}, u32[]{:S(2)}) %collective-permute-start) | collective-permute-done | bytes 524320 | tf_op jit(solution)/shard_map/ppermute | solution.py:13
  133.6 4.2 %fusion.14 = f32[1024,512]{0,1:T(8,128)} fusion(bf16[512,1024]{1,0:T(8,128)(2,1)S(1)} %pad_maximum_fusion.2, bf16[1,1024,1024]{2,1,0:T(8,128)(2,1)} %param.5), kind=kOutput, calls=%fused_computation.36 | convolution fusion | flops 1073741824 | bytes 5242880 | tf_op jit(solution)/shard_map/aq,bq->ab/dot_general | solution.py:111
  144.7 4.6 %fusion.43 = f32[1024,1024]{1,0:T(8,128)} fusion(bf16[1024,512]{0,1:T(8,128)(2,1)S(1)} %fusion.38, bf16[512,1024]{1,0:T(8,128)(2,1)} %copy-done.1), kind=kOutput, calls=%fused_computation.82 | convolution fusion | flops 1073741824 | bytes 6291456 | tf_op jit(solution)/shard_map/dot_general | solution.py:190
  149.3 4.4 %collective-permute-done.9 = bf16[256,1024]{1,0:T(8,128)(2,1)S(1)} collective-permute-done((bf16[256,1024]{1,0:T(8,128)(2,1)}, bf16[256,1024]{1,0:T(8,128)(2,1)S(1)}, u32[]{:S(2)}, u32[]{:S(2)}) %collective-permute-start.9) | collective-permute-done | bytes 524320 | tf_op jit(solution)/shard_map/ppermute | solution.py:13
  155.8 2.9 %collective-permute-done.11 = bf16[512,512]{0,1:T(8,128)(2,1)S(1)} collective-permute-done((bf16[512,512]{0,1:T(8,128)(2,1)S(1)}, bf16[512,512]{0,1:T(8,128)(2,1)S(1)}, u32[]{:S(2)}, u32[]{:S(2)}) %collective-permute-start.11) | collective-permute-done | bytes 524320 | tf_op jit(solution)/shard_map/ppermute | solution.py:127
  159.7 10.7 %reduce-scatter.9.cloned.1.call-done = f32[256,512]{0,1:T(8,128)} async-done(((f32[1024,512]{0,1:T(8,128)}), f32[256,512]{0,1:T(8,128)}) %reduce-scatter.9.cloned.1.call-update) | async-done | bytes 524304 | tf_op jit(solution)/shard_map/reduce_scatter | solution.py:114
  170.4 4.5 %fusion.17 = f32[1024,512]{0,1:T(8,128)} fusion(bf16[512,1024]{1,0:T(8,128)(2,1)} %pad_maximum_fusion.3, bf16[1,1024,1024]{2,1,0:T(8,128)(2,1)} %param.5), kind=kOutput, calls=%fused_computation.37 | convolution fusion | flops 1073741824 | bytes 5242880 | tf_op jit(solution)/shard_map/aq,bq->ab/dot_general | solution.py:111
  177.5 3.9 %collective-permute-done.12 = bf16[256,512]{0,1:T(8,128)(2,1)S(1)} collective-permute-done((bf16[256,512]{0,1:T(8,128)(2,1)S(1)}, bf16[256,512]{0,1:T(8,128)(2,1)S(1)}, u32[]{:S(2)}, u32[]{:S(2)}) %collective-permute-start.12) | collective-permute-done | bytes 262176 | tf_op jit(solution)/shard_map/ppermute | solution.py:127
  184.7 2.9 %add.128 = f32[1024,1024]{1,0:T(8,128)} add(f32[1024,1024]{1,0:T(8,128)S(1)} %copy-done, f32[1024,1024]{1,0:T(8,128)S(1)} %fusion.44) | non-fusion elementwise | flops 1048576 | bytes 12582912 | tf_op jit(solution)/shard_map/add | solution.py:191
  187.6 9.6 %collective-permute-done.13 = bf16[512,512]{0,1:T(8,128)(2,1)S(1)} collective-permute-done((bf16[512,512]{0,1:T(8,128)(2,1)S(1)}, bf16[512,512]{0,1:T(8,128)(2,1)S(1)}, u32[]{:S(2)}, u32[]{:S(2)}) %collective-permute-start.13) | collective-permute-done | bytes 524320 | tf_op jit(solution)/shard_map/ppermute | solution.py:127
  198.1 10.4 %reduce-scatter.11.cloned.1.call-done = f32[256,512]{0,1:T(8,128)} async-done(((f32[1024,512]{0,1:T(8,128)}), f32[256,512]{0,1:T(8,128)}) %reduce-scatter.11.cloned.1.call-update) | async-done | bytes 524304 | tf_op jit(solution)/shard_map/reduce_scatter | solution.py:114
  210.1 3.9 %collective-permute-done.14 = bf16[256,512]{0,1:T(8,128)(2,1)S(1)} collective-permute-done((bf16[256,512]{0,1:T(8,128)(2,1)S(1)}, bf16[256,512]{0,1:T(8,128)(2,1)S(1)}, u32[]{:S(2)}, u32[]{:S(2)}) %collective-permute-start.14) | collective-permute-done | bytes 262176 | tf_op jit(solution)/shard_map/ppermute | solution.py:127
  215.4 3.6 %convolution_add_fusion = f32[1024,1024]{1,0:T(8,128)S(1)} fusion(f32[1024,1024]{1,0:T(8,128)} %add.128, bf16[1024,512]{0,1:T(8,128)(2,1)S(1)} %fusion.28, bf16[512,1024]{1,0:T(8,128)(2,1)S(1)} %pad_maximum_fusion.2), kind=kOutput, calls=%fused_computation.1 | convolution fusion | flops 1074790400 | bytes 10485760 | tf_op jit(solution)/shard_map/dot_general | solution.py:190
  219.0 9.3 %collective-permute-done.15 = bf16[512,512]{0,1:T(8,128)(2,1)S(1)} collective-permute-done((bf16[512,512]{0,1:T(8,128)(2,1)S(1)}, bf16[512,512]{0,1:T(8,128)(2,1)S(1)}, u32[]{:S(2)}, u32[]{:S(2)}) %collective-permute-start.15) | collective-permute-done | bytes 524320 | tf_op jit(solution)/shard_map/ppermute | solution.py:127
  (70 shorter events, 45.5 us)
Async XLA Ops:
  6.5 88.4 %reduce-scatter.5.cloned.1.call-start = ((), (), s32[]{:S(2)}) async-start(), calls=%async_computation.4 | async-start | bytes 2621440 | tf_op jit(solution)/shard_map/reduce_scatter | solution.py:114
  9.3 53.5 %copy-start.2 = (bf16[1,1024,1024]{2,1,0:T(8,128)(2,1)S(1)}, bf16[1,1024,1024]{2,1,0:T(8,128)(2,1)}, u32[]{:S(2)}) copy-start(bf16[1,1024,1024]{2,1,0:T(8,128)(2,1)} %param.5) | copy-start | bytes 6291460
  9.3 27.2 %collective-permute-start.3 = (bf16[256,1024]{1,0:T(8,128)(2,1)S(1)}, bf16[256,1024]{1,0:T(8,128)(2,1)S(1)}, u32[]{:S(2)}, u32[]{:S(2)}) collective-permute-start(bf16[256,1024]{1,0:T(8,128)(2,1)S(1)} %get-tuple-element.42), channel_id=1, source_target_pairs={{0,16},{8,24},{16,0},{24,8},{1,17},{9,25},{17,1},{25,9},{2,18},{10... | collective-permute-start | bytes 1572872 | tf_op jit(solution)/shard_map/ppermute | solution.py:13
  36.5 13.1 %collective-permute-start.4 = (bf16[256,1024]{1,0:T(8,128)(2,1)S(1)}, bf16[256,1024]{1,0:T(8,128)(2,1)S(1)}, u32[]{:S(2)}, u32[]{:S(2)}) collective-permute-start(bf16[256,1024]{1,0:T(8,128)(2,1)S(1)} %collective-permute-done.3), channel_id=1, source_target_pairs={{0,1},{1,0},{2,3},{3,2},{4,5},{5,4},{6,7},{7,6},{8,9},{9,8},{10,11... | collective-permute-start | bytes 1572872 | tf_op jit(solution)/shard_map/ppermute | solution.py:13
  38.1 24.8 %collective-permute-start.2 = (bf16[256,1024]{1,0:T(8,128)(2,1)S(1)}, bf16[256,1024]{1,0:T(8,128)(2,1)}, u32[]{:S(2)}, u32[]{:S(2)}) collective-permute-start(bf16[256,1024]{1,0:T(8,128)(2,1)S(1)} %get-tuple-element.43), channel_id=1, source_target_pairs={{0,16},{8,24},{16,0},{24,8},{1,17},{9,25},{17,1},{25,9},{2,18},{10... | collective-permute-start | bytes 1572872 | tf_op jit(solution)/shard_map/ppermute | solution.py:13
  49.7 16.7 %copy-start.1 = (bf16[512,1024]{1,0:T(8,128)(2,1)}, bf16[512,1024]{1,0:T(8,128)(2,1)S(1)}, u32[]{:S(2)}) copy-start(bf16[512,1024]{1,0:T(8,128)(2,1)S(1)} %pad_maximum_fusion) | copy-start | bytes 3145732
  65.5 68.1 %reduce-scatter.7.cloned.1.call-start = ((), (), s32[]{:S(2)}) async-start(), calls=%async_computation.5 | async-start | bytes 2621440 | tf_op jit(solution)/shard_map/reduce_scatter | solution.py:114
  65.5 12.2 %collective-permute-start.5 = (bf16[256,1024]{1,0:T(8,128)(2,1)}, bf16[256,1024]{1,0:T(8,128)(2,1)S(1)}, u32[]{:S(2)}, u32[]{:S(2)}) collective-permute-start(bf16[256,1024]{1,0:T(8,128)(2,1)} %collective-permute-done.2), channel_id=1, source_target_pairs={{0,1},{1,0},{2,3},{3,2},{4,5},{5,4},{6,7},{7,6},{8,9},{9,8},{10,11... | collective-permute-start | bytes 1572872 | tf_op jit(solution)/shard_map/ppermute | solution.py:13
  66.3 24.3 %collective-permute-start.1 = (bf16[256,1024]{1,0:T(8,128)(2,1)}, bf16[256,1024]{1,0:T(8,128)(2,1)}, u32[]{:S(2)}, u32[]{:S(2)}) collective-permute-start(bf16[256,1024]{1,0:T(8,128)(2,1)} %get-tuple-element.44), channel_id=1, source_target_pairs={{0,16},{8,24},{16,0},{24,8},{1,17},{9,25},{17,1},{25,9},{2,18},{10... | collective-permute-start | bytes 1572872 | tf_op jit(solution)/shard_map/ppermute | solution.py:13
  97.5 72.8 %reduce-scatter.9.cloned.1.call-start = ((), (), s32[]{:S(2)}) async-start(), calls=%async_computation.6 | async-start | bytes 2621440 | tf_op jit(solution)/shard_map/reduce_scatter | solution.py:114
  100.2 3.9 %collective-permute-start.7 = (bf16[256,512]{0,1:T(8,128)(2,1)S(1)}, bf16[256,512]{0,1:T(8,128)(2,1)S(1)}, u32[]{:S(2)}, u32[]{:S(2)}) collective-permute-start(bf16[256,512]{0,1:T(8,128)(2,1)S(1)} %divide_convert_fusion.3), channel_id=1, source_target_pairs={{0,6},{2,0},{4,2},{6,4},{1,7},{3,1},{5,3},{7,5},{8,14},{10,8},{12,... | collective-permute-start | bytes 786440 | tf_op jit(solution)/shard_map/ppermute | solution.py:127
  100.3 14.6 %collective-permute-start.6 = (bf16[256,1024]{1,0:T(8,128)(2,1)}, bf16[256,1024]{1,0:T(8,128)(2,1)S(1)}, u32[]{:S(2)}, u32[]{:S(2)}) collective-permute-start(bf16[256,1024]{1,0:T(8,128)(2,1)} %collective-permute-done.1), channel_id=1, source_target_pairs={{0,1},{1,0},{2,3},{3,2},{4,5},{5,4},{6,7},{7,6},{8,9},{9,8},{10,11... | collective-permute-start | bytes 1572872 | tf_op jit(solution)/shard_map/ppermute | solution.py:13
  104.9 17.6 %collective-permute-start.8 = (bf16[512,512]{0,1:T(8,128)(2,1)S(1)}, bf16[512,512]{0,1:T(8,128)(2,1)}, u32[]{:S(2)}, u32[]{:S(2)}) collective-permute-start(bf16[512,512]{0,1:T(8,128)(2,1)S(1)} %pad_maximum_fusion.4), channel_id=1, source_target_pairs={{0,4},{2,6},{4,0},{6,2},{1,5},{3,7},{5,1},{7,3},{8,12},{10,14},{12... | collective-permute-start | bytes 1572872 | tf_op jit(solution)/shard_map/ppermute | solution.py:127
  106.5 27.1 %collective-permute-start = (bf16[256,1024]{1,0:T(8,128)(2,1)}, bf16[256,1024]{1,0:T(8,128)(2,1)}, u32[]{:S(2)}, u32[]{:S(2)}) collective-permute-start(bf16[256,1024]{1,0:T(8,128)(2,1)} %get-tuple-element.45), channel_id=1, source_target_pairs={{0,16},{8,24},{16,0},{24,8},{1,17},{9,25},{17,1},{25,9},{2,18},{10... | collective-permute-start | bytes 1572872 | tf_op jit(solution)/shard_map/ppermute | solution.py:13
  108.9 13.7 %copy-start.5 = (bf16[256,512]{0,1:T(8,128)(2,1)S(1)}, bf16[256,512]{0,1:T(8,128)(2,1)}, u32[]{:S(2)}) copy-start(bf16[256,512]{0,1:T(8,128)(2,1)} %copy-done.4) | copy-start | bytes 786436
  137.8 70.7 %reduce-scatter.11.cloned.1.call-start = ((), (), s32[]{:S(2)}) async-start(), calls=%async_computation.7 | async-start | bytes 2621440 | tf_op jit(solution)/shard_map/reduce_scatter | solution.py:114
  139.1 4.0 %collective-permute-start.10 = (bf16[256,512]{0,1:T(8,128)(2,1)S(1)}, bf16[256,512]{0,1:T(8,128)(2,1)S(1)}, u32[]{:S(2)}, u32[]{:S(2)}) collective-permute-start(bf16[256,512]{0,1:T(8,128)(2,1)S(1)} %divide_convert_fusion.2), channel_id=1, source_target_pairs={{0,6},{2,0},{4,2},{6,4},{1,7},{3,1},{5,3},{7,5},{8,14},{10,8},{12,... | collective-permute-start | bytes 786440 | tf_op jit(solution)/shard_map/ppermute | solution.py:127
  139.2 14.5 %collective-permute-start.9 = (bf16[256,1024]{1,0:T(8,128)(2,1)}, bf16[256,1024]{1,0:T(8,128)(2,1)S(1)}, u32[]{:S(2)}, u32[]{:S(2)}) collective-permute-start(bf16[256,1024]{1,0:T(8,128)(2,1)} %collective-permute-done), channel_id=1, source_target_pairs={{0,1},{1,0},{2,3},{3,2},{4,5},{5,4},{6,7},{7,6},{8,9},{9,8},{10,11... | collective-permute-start | bytes 1572872 | tf_op jit(solution)/shard_map/ppermute | solution.py:13
  143.2 15.6 %collective-permute-start.11 = (bf16[512,512]{0,1:T(8,128)(2,1)S(1)}, bf16[512,512]{0,1:T(8,128)(2,1)S(1)}, u32[]{:S(2)}, u32[]{:S(2)}) collective-permute-start(bf16[512,512]{0,1:T(8,128)(2,1)S(1)} %pad_maximum_fusion.5), channel_id=1, source_target_pairs={{0,4},{2,6},{4,0},{6,2},{1,5},{3,7},{5,1},{7,3},{8,12},{10,14},{12... | collective-permute-start | bytes 1572872 | tf_op jit(solution)/shard_map/ppermute | solution.py:127
  176.1 5.3 %collective-permute-start.12 = (bf16[256,512]{0,1:T(8,128)(2,1)S(1)}, bf16[256,512]{0,1:T(8,128)(2,1)S(1)}, u32[]{:S(2)}, u32[]{:S(2)}) collective-permute-start(bf16[256,512]{0,1:T(8,128)(2,1)S(1)} %divide_convert_fusion.1), channel_id=1, source_target_pairs={{0,6},{2,0},{4,2},{6,4},{1,7},{3,1},{5,3},{7,5},{8,14},{10,8},{12,... | collective-permute-start | bytes 786440 | tf_op jit(solution)/shard_map/ppermute | solution.py:127
  181.5 15.7 %collective-permute-start.13 = (bf16[512,512]{0,1:T(8,128)(2,1)S(1)}, bf16[512,512]{0,1:T(8,128)(2,1)S(1)}, u32[]{:S(2)}, u32[]{:S(2)}) collective-permute-start(bf16[512,512]{0,1:T(8,128)(2,1)S(1)} %pad_maximum_fusion.6), channel_id=1, source_target_pairs={{0,4},{2,6},{4,0},{6,2},{1,5},{3,7},{5,1},{7,3},{8,12},{10,14},{12... | collective-permute-start | bytes 1572872 | tf_op jit(solution)/shard_map/ppermute | solution.py:127
  209.7 4.3 %collective-permute-start.14 = (bf16[256,512]{0,1:T(8,128)(2,1)S(1)}, bf16[256,512]{0,1:T(8,128)(2,1)S(1)}, u32[]{:S(2)}, u32[]{:S(2)}) collective-permute-start(bf16[256,512]{0,1:T(8,128)(2,1)S(1)} %divide_convert_fusion), channel_id=1, source_target_pairs={{0,6},{2,0},{4,2},{6,4},{1,7},{3,1},{5,3},{7,5},{8,14},{10,8},{12,... | collective-permute-start | bytes 786440 | tf_op jit(solution)/shard_map/ppermute | solution.py:127
  214.0 14.3 %collective-permute-start.15 = (bf16[512,512]{0,1:T(8,128)(2,1)S(1)}, bf16[512,512]{0,1:T(8,128)(2,1)S(1)}, u32[]{:S(2)}, u32[]{:S(2)}) collective-permute-start(bf16[512,512]{0,1:T(8,128)(2,1)S(1)} %pad_maximum_fusion.7), channel_id=1, source_target_pairs={{0,4},{2,6},{4,0},{6,2},{1,5},{3,7},{5,1},{7,3},{8,12},{10,14},{12... | collective-permute-start | bytes 1572872 | tf_op jit(solution)/shard_map/ppermute | solution.py:127
  219.0 10.3 %copy-start.3 = (bf16[512,1024]{1,0:T(8,128)(2,1)S(1)}, bf16[512,1024]{1,0:T(8,128)(2,1)}, u32[]{:S(2)}) copy-start(bf16[512,1024]{1,0:T(8,128)(2,1)} %pad_maximum_fusion.3) | copy-start | bytes 3145732
  (5 other events, 9.0 us)
Sparse Core Ops, SparseCore 0:
  65.6 29.2 reduce-scatter.4
  97.7 34.4 reduce-scatter.6
  137.9 32.3 reduce-scatter.8
  175.0 33.4 reduce-scatter.10
